TPU v7x, 256 devices: a whole 4x4x8 slice. The times are simulated.
256 devices in a mesh: req: 32 (over x, y, core), kv: 8 (over z).
Axes of the slice: x: 4, y: 4, z: 8, core: 2. Of those that a mesh axis runs over, the one named last changes fastest.
Arguments:
- hidden: bfloat16 [512, 1536], P('req'), may hold values from -6 to 6
- norm_gain: float32 [1536], replicated, may hold values from 0.5 to 1.5
- w_qkv: bfloat16 [1536, 3072], P(None, 'kv'), may hold values from -0.15625 to 0.15625
- w_out: bfloat16 [1536, 1536], P(None, 'kv'), may hold values from -0.15625 to 0.15625
- cache_pages: bfloat16 [6144, 2, 8, 96, 128], P('req', None, 'kv'), may hold values from -340 to 340
- lengths: int32 [512], P('req'), may hold values from 1 to 16384, as said below
- page_table: int32 [512, 128], P('req'), may hold values from 0 to 191, as said below
- occupant: int32 [512], replicated, may hold values from 0 to 511, each once
Outputs:
- mixed: bfloat16 [512, 1536], P('req', 'kv')
Inputs may be any that keep to these rules, and one draw needn't show every extreme that they name: `occupant`: every request is served at exactly one slot. Slot s holds ceil(lengths[s] / 128) pages; on every index of req the pages of its 16 slots fit its pool of 192, some pool is full, and some request has 16384 tokens. `page_table`: the first ceil(lengths[s] / 128) entries of slot s are pages of its own pool that no other slot of that pool uses; later entries are arbitrary pages of the pool.
All inputs are finite; a program needn't handle non-finite values.
Results may differ from a plain program's by a relative error of at most 0.0043.
Values may be sent and summed in bfloat16 or wider, within the bound.
No kernel may reach another device: no remote copies, remote signals or barrier semaphores. Data moves between devices by JAX's collectives and lax.ppermute only.
A program may use at most 64 MiB of HBM per device.

v0:
```python
import math
import jax
import jax.numpy as jnp
from jax import lax
from jax.sharding import PartitionSpec as P

HD = 96
PAGE = 128
MAXP = 128
GROUP = 2


def per_device(hidden, norm_gain, w_qkv, w_out, cache_pages, lengths, page_table, occupant):
    slot_count = hidden.shape[0]
    pool_size = cache_pages.shape[0]
    kv_local = cache_pages.shape[2]
    first_slot = lax.axis_index("req") * slot_count
    hidden_wide = hidden.astype(jnp.float32)
    normed = (
        hidden_wide
        * lax.rsqrt(jnp.mean(hidden_wide * hidden_wide, axis=1, keepdims=True) + 1e-05)
        * norm_gain
    ).astype(jnp.bfloat16)
    served = lax.dynamic_slice_in_dim(occupant, first_slot, slot_count)
    every_normed = lax.all_gather(normed, "req", axis=0, tiled=True)
    picked = jnp.take(every_normed, served, axis=0)
    slot_rows = jnp.dot(picked, w_qkv, preferred_element_type=jnp.float32).astype(jnp.bfloat16)
    slot_rows = slot_rows.reshape(slot_count, kv_local, GROUP + 2, HD)
    queries = slot_rows[:, :, :GROUP]
    own_key = slot_rows[:, :, GROUP]
    own_value = slot_rows[:, :, GROUP + 1]
    score_scale = 1.0 / math.sqrt(HD)
    pages_used = (lengths + PAGE - 1) // PAGE
    live_page = jnp.arange(MAXP, dtype=jnp.int32)[None, :] < pages_used[:, None]
    matches = (
        (page_table[:, :, None] == jnp.arange(pool_size, dtype=jnp.int32)[None, None, :])
        & live_page[:, :, None]
    ).astype(jnp.int32)
    owner_table = jnp.sum(matches, axis=1)
    slot_ids = jnp.arange(slot_count, dtype=jnp.int32)
    page_owner = jnp.sum(owner_table * slot_ids[:, None], axis=0)
    page_rank = jnp.sum(matches * jnp.arange(MAXP, dtype=jnp.int32)[None, :, None], axis=(0, 1))
    page_limit = jnp.sum(owner_table * lengths[:, None], axis=0)
    offsets = page_rank[:, None] * PAGE + jnp.arange(PAGE, dtype=jnp.int32)[None, :]
    token_live = offsets < page_limit[:, None]
    page_queries = jnp.take(queries, page_owner, axis=0)
    scores = (
        jnp.einsum(
            "pgjd,pgdt->pgjt", page_queries, cache_pages[:, 0], preferred_element_type=jnp.float32
        )
        * score_scale
    )
    scores = jnp.where(token_live[:, None, None, :], scores, -jnp.inf)
    page_max = jnp.max(scores, axis=-1)
    own_score = (
        jnp.sum(queries.astype(jnp.float32) * own_key.astype(jnp.float32)[:, :, None, :], axis=-1)
        * score_scale
    )
    owner_mask = owner_table > 0
    slot_max = jnp.max(jnp.where(owner_mask[:, :, None, None], page_max[None], -jnp.inf), axis=1)
    slot_max = jnp.maximum(slot_max, own_score)
    weights = jnp.exp(scores - jnp.take(slot_max, page_owner, axis=0)[..., None])
    rounded = weights.astype(jnp.bfloat16)
    page_total = jnp.sum(weights, axis=-1)
    page_numerator = jnp.einsum(
        "pgjt,pgdt->pgjd", rounded, cache_pages[:, 1], preferred_element_type=jnp.float32
    )
    own_weight = jnp.exp(own_score - slot_max)
    own_rounded = lax.optimization_barrier(own_weight.astype(jnp.bfloat16)).astype(jnp.float32)
    owner_float = owner_table.astype(jnp.float32)
    denominator = (
        jnp.einsum("sp,pgj->sgj", owner_float, page_total, precision=lax.Precision.HIGHEST)
        + own_weight
    )
    numerator = jnp.einsum(
        "sp,pgjd->sgjd", owner_float, page_numerator, precision=lax.Precision.HIGHEST
    )
    numerator = numerator + own_rounded[..., None] * own_value.astype(jnp.float32)[:, :, None, :]
    context = (numerator / denominator[..., None]).astype(jnp.bfloat16).reshape(slot_count, -1)
    gathered = lax.all_gather(context, "req", axis=0, tiled=True)
    wanted = first_slot + slot_ids
    selector = (occupant[None, :] == wanted[:, None]).astype(jnp.bfloat16)
    attended = jnp.dot(selector, gathered, preferred_element_type=jnp.float32).astype(jnp.bfloat16)
    partial_value = lax.dot_general(
        attended, w_out, (((1,), (1,)), ((), ())), preferred_element_type=jnp.float32
    )
    summed = lax.psum_scatter(partial_value, "kv", scatter_dimension=1, tiled=True)
    col_share = summed.shape[1]
    residual = lax.dynamic_slice_in_dim(hidden_wide, lax.axis_index("kv") * col_share, col_share, 1)
    return (residual + summed).astype(jnp.bfloat16)


def solution(mesh):
    return jax.shard_map(
        per_device,
        mesh=mesh,
        in_specs=(
            P("req", None),
            P(),
            P(None, "kv"),
            P(None, "kv"),
            P("req", None, "kv", None, None),
            P("req"),
            P("req", None),
            P(),
        ),
        out_specs=P("req", "kv"),
        check_vma=False,
    )
```

profile of v0, /device:TPU:2, one launch (start us, length us, event | category | flops | bytes accessed | tf_op | source)
XLA Modules:
  0.0 147.1 jit_solution(2917014156746804395)
XLA Ops:
  6.5 1.0 multiply_reduce_fusion
  7.6 1.5 %multiply_convert_fusion = bf16[16,1536]{1,0:T(8,128)(2,1)} fusion(f32[1536]{0:T(1024)} %param.9, f32[16]{0:T(128)S(1)} %add_rsqrt_fusion, bf16[16,1536]{1,0:T(8,128)(2,1)} %param.8), kind=kLoop, calls=%fused_computation.28 | loop fusion | flops 98304 | bytes 104512 | tf_op jit(solution)/shard_map/convert_element_type | solution.py:23
  9.2 0.8 compare_and_fusion
  10.0 0.7 and_select_fusion
  10.7 1.7 %select_reduce_fusion = (s32[192]{0:T(256)S(1)}, s32[16,192]{1,0:T(8,128)S(1)}) fusion(s32[16,128]{1,0:T(8,128)} %param.14, pred[16,128]{1,0:T(8,128)(4,1)S(1)} %iota_compare_fusion.1), kind=kLoop, calls=%fused_computation.10 | loop fusion | flops 2356032 | bytes 23296 | tf_op jit(solution)/shard_map/reduce_sum | solution.py:42
  12.4 0.7 multiply_reduce_fusion.2
  13.2 0.1 add_compare_fusion
  13.3 47.2 %all-gather.2.cloned.1.call-done = bf16[512,1536]{1,0:T(8,128)(2,1)} async-done(((bf16[16,1536]{1,0:T(8,128)(2,1)}), bf16[512,1536]{1,0:T(8,128)(2,1)}) %all-gather.2.cloned.1.call-update) | async-done | bytes 1572880 | tf_op jit(solution)/shard_map/all_gather | solution.py:25
  60.5 2.2 %gather_fusion = bf16[16,1536]{1,0:T(8,128)(2,1)S(1)} fusion(bf16[512,1536]{1,0:T(8,128)(2,1)} %all-gather.2.cloned.1.call-done, s32[1024]{0:T(1024)S(1)} %pad_clamp_fusion.1), kind=kCustom, calls=%fused_computation | custom fusion | bytes 98368 | tf_op jit(solution)/shard_map/jit(_take)/gather | solution.py:26
  62.7 0.3 convolution_convert_fusion
  63.2 0.1 multiply_reduce_fusion.1
  63.4 0.8 gather_fusion.1
  64.2 3.8 %fusion.39 = (f32[192,2]{1,0:T(8,128)S(1)}, f32[192,2,128]{2,1,0:T(2,128)S(1)}) fusion(bf16[192,2,1,96,128]{4,3,2,1,0:T(8,128)(2,1)} %param.12, bf16[192,2,96]{2,1,0:T(2,128)(2,1)S(1)} %gather_fusion.1, pred[192]{0:T(512)(128)(4,1)S(1)} %compare_and_fusion.1, pred[192,128]{1,0:T(8,128)(4,1)S(1)} %add_compare_fusion), kind=kOutput, calls=%fused_computation.76 | convolution fusion | flops 9621120 | bytes 5015232 | tf_op jit(solution)/shard_map/pgjd,pgdt->pgjt/dot_general | solution.py:48
  68.2 0.1 select_reduce_fusion.1
  68.4 0.7 gather_fusion.2
  69.2 5.0 %fusion = f32[192,2,96]{2,1,0:T(2,128)S(1)} fusion(bf16[192,2,1,96,128]{4,3,2,1,0:T(8,128)(2,1)} %param.12, f32[192,2,128]{2,1,0:T(2,128)S(1)} %get-tuple-element.16, f32[192,2]{1,0:T(8,128)S(1)} %broadcast_select_fusion.2), kind=kOutput, calls=%fused_computation.3 | convolution fusion | flops 9535488 | bytes 5064192 | tf_op jit(solution)/shard_map/pgjt,pgdt->pgjd/dot_general | solution.py:65
  74.2 0.5 fusion.16
  74.8 0.3 convolution_add_fusion.1
  75.0 0.3 fusion.11
  75.4 23.2 %all_gather.7 = bf16[512,192]{1,0:T(8,128)(2,1)S(1)} all-gather(bf16[16,192]{1,0:T(8,128)(2,1)S(1)} %reshape.233), channel_id=1, replica_groups=mesh['req'=32,'kv'=8] {'req'}, dimensions={0}, use_global_device_ids=true | all-gather | bytes 202752 | tf_op jit(solution)/shard_map/all_gather | solution.py:80
  98.6 1.5 %convolution_bitcast_fusion = f32[1536,16]{1,0:T(8,128)} fusion(bf16[1536,192]{0,1:T(8,128)(2,1)S(1)} %copy-done.1, bf16[512,192]{1,0:T(8,128)(2,1)S(1)} %all_gather.7, s32[512]{0:T(512)S(1)} %copy-done.3, s32[16]{0:T(128)S(1)} %iota_add_fusion), kind=kOutput, calls=%fused_computation.9 | convolution fusion | flops 12594176 | bytes 886848
  100.2 38.5 %reduce-scatter.4.cloned.1.call-done = f32[192,16]{1,0:T(8,128)} async-done(((f32[1536,16]{1,0:T(8,128)}), f32[192,16]{1,0:T(8,128)}) %reduce-scatter.4.cloned.1.call-update) | async-done | bytes 12304
  138.6 0.9 copy.34
  139.6 0.7 add_convert_fusion
  (33 shorter events, 0.8 us)
Async XLA Ops:
  6.5 56.2 %copy-start = (bf16[1536,384]{1,0:T(8,128)(2,1)S(1)}, bf16[1536,384]{1,0:T(8,128)(2,1)}, u32[]{:S(2)}) copy-start(bf16[1536,384]{1,0:T(8,128)(2,1)} %param.10) | copy-start | bytes 3538948
  6.5 53.9 %all-gather.2.cloned.1.call-start = ((), (), s32[]{:S(2)}) async-start(), calls=%async_computation.1 | async-start | bytes 1622016 | tf_op jit(solution)/shard_map/all_gather | solution.py:25
  9.1 129.5 %reduce-scatter.4.cloned.1.call-start = ((), (), s32[]{:S(2)}) async-start(), calls=%async_computation.2 | async-start | bytes 884736
  69.2 29.5 %copy-start.1 = (bf16[1536,192]{0,1:T(8,128)(2,1)S(1)}, bf16[1536,192]{0,1:T(8,128)(2,1)}, u32[]{:S(2)}) copy-start(bf16[1536,192]{0,1:T(8,128)(2,1)} %param.11) | copy-start | bytes 1769476
  69.2 29.4 %copy-start.3 = (s32[512]{0:T(512)S(1)}, s32[512]{0:T(512)}, u32[]{:S(2)}) copy-start(s32[512]{0:T(512)} %param.15) | copy-start | bytes 6148
  74.7 25.4 %copy-start.2 = (bf16[16,1536]{1,0:T(8,128)(2,1)S(1)}, bf16[16,1536]{1,0:T(8,128)(2,1)}, u32[]{:S(2)}) copy-start(bf16[16,1536]{1,0:T(8,128)(2,1)} %param.8) | copy-start | bytes 147460
Sparse Core Ops, SparseCore 0:
  9.9 50.5 all-gather.1
  100.2 38.3 reduce-scatter.3
where the time goes:
time: 147 us
  waiting for transfers between devices  85.7 us (58%)
  blocking collectives  23.2 us (16%)
  between operations  13.6 us (9%)
  matrix products  11.2 us (8%)
  other arithmetic  8.17 us (6%)
  local copies, waits for them, and re-layouts  5.21 us (4%)
    all_gather x1, waiting for transfers between devices, per_device(): every_normed = lax.all_gather(normed, 'req', axis=0, tiled=True)  47.2 us
    unnamed x3, waiting for transfers between devices  38.5 us
    all_gather x1, blocking collectives, per_device(): gathered = lax.all_gather(context, 'req', axis=0, tiled=True)  23.2 us
    dot_general x1, matrix products, per_device(): jnp.einsum('pgjt,pgdt->pgjd', rounded, cache_pages[:, 1], preferred_eleme...  5.01 us
    dot_general x1, matrix products, per_device(): jnp.einsum('pgjd,pgdt->pgjt', page_queries, cache_pages[:, 0], preferred_...  3.85 us
  transfers between devices with their start and end apart: 2, of which 2 were waited for; matrix products, arithmetic and copies ran while one was open for 3% of the time, Pallas kernels for 0%

commit v1 on v0

--- a/solution.py
+++ b/solution.py
@@ -22,7 +22,9 @@
         * norm_gain
     ).astype(jnp.bfloat16)
     served = lax.dynamic_slice_in_dim(occupant, first_slot, slot_count)
-    every_normed = lax.all_gather(normed, "req", axis=0, tiled=True)
+    every_normed = jnp.concatenate(
+        lax.all_to_all(jnp.stack([normed] * lax.axis_size("req")), "req", 0, 0), axis=0
+    )
     picked = jnp.take(every_normed, served, axis=0)
     slot_rows = jnp.dot(picked, w_qkv, preferred_element_type=jnp.float32).astype(jnp.bfloat16)
     slot_rows = slot_rows.reshape(slot_count, kv_local, GROUP + 2, HD)

time: 147 us -> 125 us (0.85)
  waiting for transfers between devices: 85.7 us -> 57.9 us
  starting transfers between devices: 0.04 us -> 7.8 us
  other arithmetic: 8.17 us -> 4.88 us
  blocking collectives: 23.2 us -> 24.9 us
    all_gather x1 -> x0, waiting for transfers between devices: 47.2 us -> none  [per_device(): every_normed = lax.all_gather(normed, 'req', axis=0, tiled=True)]
    all_to_all x0 -> x1, waiting for transfers between devices: none -> 18.6 us  [per_device(): lax.all_to_all(jnp.stack([normed] * lax.axis_size('req')), 'req', 0, 0)]
    all_to_all x0 -> x1, starting transfers between devices: none -> 7.75 us  [per_device(): lax.all_to_all(jnp.stack([normed] * lax.axis_size('req')), 'req', 0, 0)]
    gather x1, local copies, waits for them, and re-layouts: 2.25 us -> 0.59 us  [per_device(): picked = jnp.take(every_normed, served, axis=0)]
    all_gather x1, blocking collectives: 23.2 us -> 24.9 us  [per_device(): gathered = lax.all_gather(context, 'req', axis=0, tiled=True)]
    unnamed x3 -> x2, waiting for transfers between devices: 38.5 us -> 39.3 us
  transfers between devices with their start and end apart: 2 -> 2, of which waited for: 2 -> 2; matrix products, arithmetic and copies ran while one was open for 3% -> 1% of each run, Pallas kernels for 0% -> 0%
where the time goes in v1:
time: 125 us
  waiting for transfers between devices  57.9 us (46%)
  blocking collectives  24.9 us (20%)
  between operations  13.6 us (11%)
  matrix products  11.2 us (9%)
  starting transfers between devices  7.8 us (6%)
  local copies, waits for them, and re-layouts  4.89 us (4%)
  other arithmetic  4.88 us (4%)
    unnamed x2, waiting for transfers between devices  39.3 us
    all_gather x1, blocking collectives, per_device(): gathered = lax.all_gather(context, 'req', axis=0, tiled=True)  24.9 us
    all_to_all x1, waiting for transfers between devices, per_device(): lax.all_to_all(jnp.stack([normed] * lax.axis_size('req')), 'req', 0, 0)  18.6 us
    all_to_all x1, starting transfers between devices, per_device(): lax.all_to_all(jnp.stack([normed] * lax.axis_size('req')), 'req', 0, 0)  7.75 us
    dot_general x1, matrix products, per_device(): jnp.einsum('pgjt,pgdt->pgjd', rounded, cache_pages[:, 1], preferred_eleme...  5.01 us
    dot_general x1, matrix products, per_device(): jnp.einsum('pgjd,pgdt->pgjt', page_queries, cache_pages[:, 0], preferred_...  3.84 us
  transfers between devices with their start and end apart: 2, of which 2 were waited for; matrix products, arithmetic and copies ran while one was open for 1% of the time, Pallas kernels for 0%

profile of v1, /device:TPU:2, one launch (start us, length us, event | category | flops | bytes accessed | tf_op | source)
XLA Modules:
  0.0 125.1 jit_solution(12680022186596960200)
XLA Ops:
  6.5 1.0 multiply_reduce_fusion
  7.6 0.9 multiply_convert_fusion
  8.5 1.3 %stack.2 = bf16[32,16,1536]{2,1,0:T(8,128)(2,1)} broadcast(bf16[16,1536]{1,0:T(8,128)(2,1)S(1)} %multiply_convert_fusion), dimensions={1,2} | broadcast | bytes 1622016 | tf_op jit(solution)/shard_map/stack | solution.py:26
  9.8 7.8 %all-to-all-start = ((bf16[32,16,1536]{2,1,0:T(8,128)(2,1)}), bf16[32,16,1536]{2,1,0:T(8,128)(2,1)S(1)}, u32[]{:S(2)}, u32[]{:S(2)}) async-start(bf16[32,16,1536]{2,1,0:T(8,128)(2,1)} %stack.2), calls=%async_computation | async-start | bytes 3145728 | tf_op jit(solution)/shard_map/all_to_all | solution.py:26
  17.8 1.0 select_reduce_fusion
  19.0 0.1 add_compare_fusion
  19.1 18.6 %all-to-all-done = bf16[32,16,1536]{2,1,0:T(8,128)(2,1)S(1)} async-done(((bf16[32,16,1536]{2,1,0:T(8,128)(2,1)}), bf16[32,16,1536]{2,1,0:T(8,128)(2,1)S(1)}, u32[]{:S(2)}, u32[]{:S(2)}) %all-to-all-start) | async-done | bytes 1572896 | tf_op jit(solution)/shard_map/all_to_all | solution.py:26
  37.7 0.6 gather_fusion
  38.3 0.3 convolution_convert_fusion
  38.8 0.1 multiply_reduce_fusion.1
  38.9 0.8 gather_fusion.1
  39.8 3.8 %fusion.39 = (f32[192,2]{1,0:T(8,128)S(1)}, f32[192,2,128]{2,1,0:T(2,128)S(1)}) fusion(bf16[192,2,1,96,128]{4,3,2,1,0:T(8,128)(2,1)} %param.12, bf16[192,2,96]{2,1,0:T(2,128)(2,1)S(1)} %gather_fusion.1, pred[192]{0:T(512)(128)(4,1)S(1)} %compare_and_fusion.1, pred[192,128]{1,0:T(8,128)(4,1)S(1)} %add_compare_fusion), kind=kOutput, calls=%fused_computation.76 | convolution fusion | flops 9621120 | bytes 5015232 | tf_op jit(solution)/shard_map/pgjd,pgdt->pgjt/dot_general | solution.py:50
  43.7 0.1 select_reduce_fusion.1
  43.9 0.7 gather_fusion.2
  44.6 0.1 broadcast_select_fusion.2
  44.7 5.0 %fusion = f32[192,2,96]{2,1,0:T(2,128)S(1)} fusion(bf16[192,2,1,96,128]{4,3,2,1,0:T(8,128)(2,1)} %param.12, f32[192,2,128]{2,1,0:T(2,128)S(1)} %get-tuple-element.16, f32[192,2]{1,0:T(8,128)S(1)} %broadcast_select_fusion.2), kind=kOutput, calls=%fused_computation.3 | convolution fusion | flops 9535488 | bytes 5064192 | tf_op jit(solution)/shard_map/pgjt,pgdt->pgjd/dot_general | solution.py:67
  49.7 0.5 fusion.16
  50.3 0.3 convolution_add_fusion.1
  50.5 0.3 fusion.11
  50.9 24.9 %all_gather.3 = bf16[512,192]{1,0:T(8,128)(2,1)S(1)} all-gather(bf16[16,192]{1,0:T(8,128)(2,1)S(1)} %reshape.239), channel_id=1, replica_groups=mesh['req'=32,'kv'=8] {'req'}, dimensions={0}, use_global_device_ids=true | all-gather | bytes 202752 | tf_op jit(solution)/shard_map/all_gather | solution.py:82
  75.8 1.5 %convolution_bitcast_fusion = f32[1536,16]{1,0:T(8,128)} fusion(bf16[1536,192]{0,1:T(8,128)(2,1)S(1)} %copy-done.1, bf16[512,192]{1,0:T(8,128)(2,1)S(1)} %all_gather.3, s32[512]{0:T(512)S(1)} %copy-done.4, s32[16]{0:T(128)S(1)} %iota_add_fusion), kind=kOutput, calls=%fused_computation.9 | convolution fusion | flops 12594176 | bytes 886848
  77.3 39.3 %reduce-scatter.4.cloned.1.call-done = f32[192,16]{1,0:T(8,128)} async-done(((f32[1536,16]{1,0:T(8,128)}), f32[192,16]{1,0:T(8,128)}) %reduce-scatter.4.cloned.1.call-update) | async-done | bytes 12304
  116.7 0.9 copy.34
  117.6 0.7 add_convert_fusion
  (37 shorter events, 0.9 us)
Async XLA Ops:
  6.5 31.8 %copy-start = (bf16[1536,384]{1,0:T(8,128)(2,1)S(1)}, bf16[1536,384]{1,0:T(8,128)(2,1)}, u32[]{:S(2)}) copy-start(bf16[1536,384]{1,0:T(8,128)(2,1)} %param.10) | copy-start | bytes 3538948
  9.8 7.8 %copy-start.4 = (s32[512]{0:T(512)S(1)}, s32[512]{0:T(512)}, u32[]{:S(2)}) copy-start(s32[512]{0:T(512)} %param.15) | copy-start | bytes 6148
  9.8 7.9 %copy-start.5 = (s32[16]{0:T(128)S(1)}, s32[16]{0:T(128)}, u32[]{:S(2)}) copy-start(s32[16]{0:T(128)} %param.13) | copy-start | bytes 196
  9.8 8.0 %copy-start.3 = (s32[16,128]{1,0:T(8,128)S(1)}, s32[16,128]{1,0:T(8,128)}, u32[]{:S(2)}) copy-start(s32[16,128]{1,0:T(8,128)} %param.14) | copy-start | bytes 24580
  9.8 27.9 %all-to-all-start = ((bf16[32,16,1536]{2,1,0:T(8,128)(2,1)}), bf16[32,16,1536]{2,1,0:T(8,128)(2,1)S(1)}, u32[]{:S(2)}, u32[]{:S(2)}) async-start(bf16[32,16,1536]{2,1,0:T(8,128)(2,1)} %stack.2), calls=%async_computation | async-start | bytes 3145728 | tf_op jit(solution)/shard_map/all_to_all | solution.py:26
  17.6 99.1 %reduce-scatter.4.cloned.1.call-start = ((), (), s32[]{:S(2)}) async-start(), calls=%async_computation.2 | async-start | bytes 884736
  44.7 31.1 %copy-start.1 = (bf16[1536,192]{0,1:T(8,128)(2,1)S(1)}, bf16[1536,192]{0,1:T(8,128)(2,1)}, u32[]{:S(2)}) copy-start(bf16[1536,192]{0,1:T(8,128)(2,1)} %param.11) | copy-start | bytes 1769476
  50.3 27.0 %copy-start.2 = (bf16[16,1536]{1,0:T(8,128)(2,1)S(1)}, bf16[16,1536]{1,0:T(8,128)(2,1)}, u32[]{:S(2)}) copy-start(bf16[16,1536]{1,0:T(8,128)(2,1)} %param.8) | copy-start | bytes 147460
Sparse Core Ops, SparseCore 0:
  77.4 39.1 reduce-scatter.3
